TPU v7x, 512 devices: a whole 4x8x8 slice. The times are simulated.
512 devices in a mesh: seq: 64 (over z, x, core), head: 8 (over y).
Axes of the slice: x: 4, y: 8, z: 8, core: 2. Of those that a mesh axis runs over, the one named last changes fastest.
Arguments:
- projected: float32 [65536, 2560], P(('seq', 'head')), may hold values from -6 to 6
- out_grads: float32 [65536, 2048], P(('seq', 'head')), may hold values from -6 to 6
- conv_weight: float32 [3, 2560], replicated, may hold values from -2.4 to 2.4
- doc_lengths: int32 [16], replicated, may hold values from 1 to 32768, 65536 in all
Outputs:
- grad_projected: float32 [65536, 2560], P(('seq', 'head'))
- grad_conv: float32 [3, 2560], replicated
Inputs may be any that keep to these rules, and one draw needn't show every extreme that they name: `doc_lengths`: the 16 documents fill the 65536 tokens end to end; the longest holds exactly half of 65536 tokens.
All inputs are finite; a program needn't handle non-finite values.
Results may differ from a plain program's by a relative error of at most 0.0003.
Values sent between devices are 32-bit elements; how exact they have to be, the bound alone decides.
No kernel may reach another device: no remote copies, remote signals or barrier semaphores. Data moves between devices by JAX's collectives and lax.ppermute only.
A program may use at most 128 MiB of HBM per device.

v0:
```python
import math
import jax
import jax.numpy as jnp
import numpy as np
from jax import lax
from jax.sharding import PartitionSpec as P

KEY_DIM = 16
HEAD_DIM = 128
HIGHEST = lax.Precision.HIGHEST


def segment_sum(gathered, flags, here, reverse):
    count = gathered.shape[0]
    index = jnp.arange(count, dtype=jnp.int32)
    started = flags > 0.5
    if reverse:
        bound = jnp.min(jnp.where((index > here) & started, index, count - 1))
        take = (index > here) & (index <= bound)
    else:
        bound = jnp.max(jnp.where((index < here) & started, index, 0))
        take = (index >= bound) & (index < here)
    return jnp.sum(jnp.where(take[:, None], gathered, 0.0), axis=0)


def carried_in(state, norm, extra, flags, axis, reverse):
    here = lax.axis_index(axis)
    size = state.size
    packed = jnp.concatenate([state.reshape(-1), norm.reshape(-1), extra])
    width = 128
    padded = jnp.pad(packed, (0, -packed.shape[0] % width)).reshape(-1, width)
    gathered = lax.all_gather(padded, axis).reshape(lax.axis_size(axis), -1)
    if flags is None:
        flags = gathered[:, packed.shape[0] - 1]
    total = segment_sum(gathered[:, : size + norm.size], flags, here, reverse)
    return (total[:size].reshape(state.shape), total[size:].reshape(norm.shape), flags)


def passed_along(value, axis, steps):
    count = lax.axis_size(axis)
    initial, last = (max(0, -steps), min(count, count - steps))
    return lax.ppermute(value, axis, [(source, source + steps) for source in range(initial, last)])


def feature_map(columns):
    key_size = columns.shape[1]
    upper_i, upper_j = np.triu_indices(key_size)
    factors = np.where(upper_i == upper_j, 1.0 / math.sqrt(2.0), 1.0).astype(np.float32)
    products = columns[:, upper_i, :] * columns[:, upper_j, :] * jnp.asarray(factors)[None, :, None]
    constant = jnp.ones((columns.shape[0], 1, columns.shape[2]), jnp.float32)
    return jnp.concatenate([constant, columns, products], axis=1)


def doc_place(doc_lengths, anchor, amount):
    positions = anchor + jnp.arange(amount, dtype=jnp.int32)
    starts = jnp.cumsum(doc_lengths) - doc_lengths
    begins = jnp.max(jnp.where(starts[None, :] <= positions[:, None], starts[None, :], 0), axis=1)
    return (begins, positions - begins)


def conv_forward(signal, leading, weights, offsets):
    row_count = signal.shape[0]
    behind = jnp.concatenate([leading, signal], axis=0)
    back_one = behind[1 : row_count + 1] * (offsets[0:row_count] >= 1).astype(jnp.float32)[:, None]
    back_two = behind[0:row_count] * (offsets[0:row_count] >= 2).astype(jnp.float32)[:, None]
    return weights[0] * signal + weights[1] * back_one + weights[2] * back_two


def conv_backward(grad_rows, trailing, signal, leading, weights, offsets):
    row_count = grad_rows.shape[0]
    ahead_rows = jnp.concatenate([grad_rows, trailing], axis=0)
    ahead_one = (
        ahead_rows[1 : row_count + 1]
        * (offsets[1 : row_count + 1] >= 1).astype(jnp.float32)[:, None]
    )
    ahead_two = (
        ahead_rows[2 : row_count + 2]
        * (offsets[2 : row_count + 2] >= 2).astype(jnp.float32)[:, None]
    )
    grad_signal = weights[0] * grad_rows + weights[1] * ahead_one + weights[2] * ahead_two
    behind = jnp.concatenate([leading, signal], axis=0)
    own_one = (offsets[0:row_count] >= 1).astype(jnp.float32)[:, None]
    own_two = (offsets[0:row_count] >= 2).astype(jnp.float32)[:, None]
    grad_weights = jnp.stack(
        [
            jnp.sum(grad_rows * signal, axis=0),
            jnp.sum(grad_rows * behind[1 : row_count + 1] * own_one, axis=0),
            jnp.sum(grad_rows * behind[0:row_count] * own_two, axis=0),
        ],
        axis=0,
    )
    return (grad_signal, grad_weights)


def attention_grads(mixed_rows, out_flat, begins, stretch_start):
    length = mixed_rows.shape[0]
    head_width = 2 * KEY_DIM + HEAD_DIM
    local_heads = mixed_rows.shape[1] // head_width
    block_len = min(128, length)
    blocks = length // block_len
    scale_key = KEY_DIM ** (-0.25)
    shaped = mixed_rows.reshape(length, local_heads, head_width)
    query_cols = jnp.transpose(shaped[:, :, :KEY_DIM], (1, 2, 0)) * scale_key
    key_cols = jnp.transpose(shaped[:, :, KEY_DIM : 2 * KEY_DIM], (1, 2, 0)) * scale_key
    values = shaped[:, :, 2 * KEY_DIM :]
    upstream = out_flat.reshape(length, local_heads, HEAD_DIM)
    query_feat, query_pull = jax.vjp(feature_map, query_cols)
    key_feat, key_pull = jax.vjp(feature_map, key_cols)
    feat_count = query_feat.shape[1]
    last_begin = begins[length - 1]
    has_start = (last_begin >= stretch_start).astype(jnp.float32).reshape(1)
    tail_mask = (begins == last_begin).astype(jnp.float32)
    tail_feat = key_feat * tail_mask[None, None, :]
    tail_state = jnp.einsum("hfl,lhe->hfe", tail_feat, values, precision=HIGHEST)
    tail_norm = jnp.sum(tail_feat, axis=2)
    prefix = carried_in(tail_state, tail_norm, has_start, None, "seq", False)
    flags = prefix[2]
    causal = jnp.arange(block_len)[:, None] >= jnp.arange(block_len)[None, :]
    indices = jnp.arange(blocks, dtype=jnp.int32)

    def forward_block(carried, block_index):
        carry_state, carry_norm = carried
        offset_rows = block_index * block_len
        block_start = stretch_start + offset_rows
        query_blk = lax.dynamic_slice_in_dim(query_feat, offset_rows, block_len, 2)
        key_blk = lax.dynamic_slice_in_dim(key_feat, offset_rows, block_len, 2)
        value_blk = lax.dynamic_slice_in_dim(values, offset_rows, block_len, 0)
        doc_blk = lax.dynamic_slice_in_dim(begins, offset_rows, block_len, 0)
        allowed = causal & (doc_blk[:, None] == doc_blk[None, :])
        scores = jnp.where(
            allowed[None], jnp.einsum("hft,hfs->hts", query_blk, key_blk, precision=HIGHEST), 0.0
        )
        from_carry = (doc_blk < block_start).astype(jnp.float32)
        numerator = jnp.einsum("hts,she->the", scores, value_blk, precision=HIGHEST) + from_carry[
            :, None, None
        ] * jnp.einsum("hft,hfe->the", query_blk, carry_state, precision=HIGHEST)
        denominator = jnp.sum(scores, axis=2) + from_carry[None, :] * jnp.einsum(
            "hft,hf->ht", query_blk, carry_norm, precision=HIGHEST
        )
        block_tail = (doc_blk == doc_blk[block_len - 1]).astype(jnp.float32)
        carry_keep = (doc_blk[block_len - 1] < block_start).astype(jnp.float32)
        tail_keys = key_blk * block_tail[None, None, :]
        next_state = (
            jnp.einsum("hfs,she->hfe", tail_keys, value_blk, precision=HIGHEST)
            + carry_keep * carry_state
        )
        next_norm = jnp.sum(tail_keys, axis=2) + carry_keep * carry_norm
        return ((next_state, next_norm), (numerator, denominator, carry_state, carry_norm, scores))

    forward_out = lax.scan(forward_block, (prefix[0], prefix[1]), indices)
    numerators, denominators, states, norms, kept_scores = forward_out[1]
    denom_rows = jnp.transpose(denominators, (0, 2, 1)).reshape(length, local_heads)
    attended = numerators.reshape(length, local_heads, HEAD_DIM) / denom_rows[:, :, None]
    grad_num = upstream / denom_rows[:, :, None]
    scalar_grad = -jnp.sum(upstream * attended, axis=2) / denom_rows
    lead_mask = (begins < stretch_start).astype(jnp.float32)
    lead_feat = query_feat * lead_mask[None, None, :]
    lead_state = jnp.einsum("hfl,lhe->hfe", lead_feat, grad_num, precision=HIGHEST)
    lead_norm = jnp.einsum("hfl,lh->hf", lead_feat, scalar_grad, precision=HIGHEST)
    suffix = carried_in(lead_state, lead_norm, jnp.zeros((0,), jnp.float32), flags, "seq", True)

    def backward_block(carried, inputs):
        back_state, back_norm = carried
        block_index, carry_state, carry_norm, scores = inputs
        offset_rows = block_index * block_len
        block_start = stretch_start + offset_rows
        query_blk = lax.dynamic_slice_in_dim(query_feat, offset_rows, block_len, 2)
        key_blk = lax.dynamic_slice_in_dim(key_feat, offset_rows, block_len, 2)
        value_blk = lax.dynamic_slice_in_dim(values, offset_rows, block_len, 0)
        doc_blk = lax.dynamic_slice_in_dim(begins, offset_rows, block_len, 0)
        grad_blk = lax.dynamic_slice_in_dim(grad_num, offset_rows, block_len, 0)
        scalar_blk = lax.dynamic_slice_in_dim(scalar_grad, offset_rows, block_len, 0)
        scalar_cols = scalar_blk.T
        allowed = causal & (doc_blk[:, None] == doc_blk[None, :])
        dscores = jnp.where(
            allowed[None],
            jnp.einsum("the,she->hts", grad_blk, value_blk, precision=HIGHEST)
            + scalar_cols[:, :, None],
            0.0,
        )
        from_carry = (doc_blk < block_start).astype(jnp.float32)
        block_tail = (doc_blk == doc_blk[block_len - 1]).astype(jnp.float32)
        carry_keep = (doc_blk[block_len - 1] < block_start).astype(jnp.float32)
        grad_query = jnp.einsum("hts,hfs->hft", dscores, key_blk, precision=HIGHEST) + from_carry[
            None, None, :
        ] * (
            jnp.einsum("hfe,the->hft", carry_state, grad_blk, precision=HIGHEST)
            + carry_norm[:, :, None] * scalar_cols[:, None, :]
        )
        grad_key = jnp.einsum("hts,hft->hfs", dscores, query_blk, precision=HIGHEST) + block_tail[
            None, None, :
        ] * (
            jnp.einsum("hfe,she->hfs", back_state, value_blk, precision=HIGHEST)
            + back_norm[:, :, None]
        )
        grad_value = jnp.einsum("hts,the->she", scores, grad_blk, precision=HIGHEST) + block_tail[
            :, None, None
        ] * jnp.einsum("hfs,hfe->she", key_blk, back_state, precision=HIGHEST)
        lead_blk = query_blk * from_carry[None, None, :]
        next_state = (
            jnp.einsum("hft,the->hfe", lead_blk, grad_blk, precision=HIGHEST)
            + carry_keep * back_state
        )
        next_norm = (
            jnp.einsum("hft,th->hf", lead_blk, scalar_blk, precision=HIGHEST)
            + carry_keep * back_norm
        )
        return ((next_state, next_norm), (grad_query, grad_key, grad_value))

    swept_back = lax.scan(
        backward_block, (suffix[0], suffix[1]), (indices, states, norms, kept_scores), reverse=True
    )
    grad_qblocks, grad_kblocks, grad_vblocks = swept_back[1]
    query_grad = jnp.transpose(grad_qblocks, (1, 2, 0, 3)).reshape(local_heads, feat_count, length)
    key_grad = jnp.transpose(grad_kblocks, (1, 2, 0, 3)).reshape(local_heads, feat_count, length)
    value_grad = grad_vblocks.reshape(length, local_heads, HEAD_DIM)
    query_in = jnp.transpose(query_pull(query_grad)[0] * scale_key, (2, 0, 1))
    key_in = jnp.transpose(key_pull(key_grad)[0] * scale_key, (2, 0, 1))
    return jnp.concatenate([query_in, key_in, value_grad], axis=2).reshape(
        length, local_heads * head_width
    )


def on_device(projected, out_grads, conv_weight, doc_lengths):
    row_count = projected.shape[0]
    head_count = lax.axis_size("head")
    seq_index = lax.axis_index("seq")
    head_index = lax.axis_index("head")
    group_len = row_count * head_count
    token_base = (seq_index * head_count + head_index) * row_count
    stretch_start = seq_index * group_len
    token_begins, token_offsets = doc_place(doc_lengths, token_base, row_count + 2)
    leading = passed_along(projected[row_count - 2 :], ("seq", "head"), 1)
    outgoing = conv_forward(projected, leading, conv_weight, token_offsets)
    arrived, upstream = (
        lax.all_to_all(outgoing, "head", split_axis=1, concat_axis=0, tiled=True),
        lax.all_to_all(out_grads, "head", split_axis=1, concat_axis=0, tiled=True),
    )
    group_begins, group_offsets = doc_place(doc_lengths, stretch_start, group_len + 2)
    grad_mixed = attention_grads(arrived, upstream, group_begins[:group_len], stretch_start)
    returned = lax.all_to_all(grad_mixed, "head", split_axis=0, concat_axis=1, tiled=True)
    trailing = passed_along(returned[:2], ("seq", "head"), -1)
    grad_projected, weight_part = conv_backward(
        returned, trailing, projected, leading, conv_weight, token_offsets
    )
    grad_conv = lax.psum(weight_part, ("seq", "head"))
    return (grad_projected, grad_conv)


def solution(mesh):
    return jax.shard_map(
        on_device,
        mesh=mesh,
        in_specs=(P(("seq", "head"), None), P(("seq", "head"), None), P(), P()),
        out_specs=(P(("seq", "head"), None), P()),
        check_vma=False,
    )
```

profile of v0, /device:TPU:1, one launch (start us, length us, event | category | flops | bytes accessed | tf_op | source)
XLA Modules:
  0.0 737.0 jit_solution(17403635177316418319)
XLA Ops:
  8.1 4.0 collective-permute-start
  14.8 1.7 copy.221
  17.0 3.1 multiply_add_fusion.1
  20.1 6.1 all-to-all-start
  28.1 32.9 %all-to-all-done = f32[128,8,320]{0,2,1:T(8,128)S(1)} async-done(((f32[128,8,320]{0,2,1:T(8,128)}), f32[128,8,320]{0,2,1:T(8,128)S(1)}, u32[]{:S(2)}, u32[]{:S(2)}) %all-to-all-start) | async-done | bytes 1310752 | tf_op jit(solution)/shard_map/all_to_all | solution.py:236
  61.0 1.8 copy.225
  62.8 2.0 reshape.227
  65.0 3.0 gather_fusion
  68.1 3.1 gather_fusion.1
  71.1 3.0 gather_fusion.2
  74.2 3.0 gather_fusion.3
  77.2 3.4 fusion.89
  80.6 4.3 fusion.98
  88.8 3.6 all-to-all-start.1
  92.7 28.9 %all-to-all-done.1 = f32[128,8,256]{0,2,1:T(8,128)S(1)} async-done(((f32[128,8,256]{0,2,1:T(8,128)}), f32[128,8,256]{0,2,1:T(8,128)S(1)}, u32[]{:S(2)}, u32[]{:S(2)}) %all-to-all-start.1) | async-done | bytes 1048608 | tf_op jit(solution)/shard_map/all_to_all | solution.py:237
  123.2 2.4 reshape.233
  128.4 2.5 copy.272
  131.0 48.2 %all-gather.3.cloned.1.call-done = f32[64,309,128]{2,1,0:T(8,128)} async-done(((f32[1,309,128]{2,1,0:T(8,128)}), f32[64,309,128]{2,1,0:T(8,128)}) %all-gather.3.cloned.1.call-update) | async-done | bytes 10125328 | tf_op jit(solution)/shard_map/all_gather | solution.py:32
  179.2 5.7 copy.305
  188.8 110.3 %while.46 = (s32[]{:T(128)}, f32[2,153,128]{2,1,0:T(8,128)S(1)}, f32[2,153]{1,0:T(2,128)S(1)}, f32[8,128,2,128]{1,0,3,2:T(8,128)}, f32[8,2,128]{2,1,0:T(2,128)S(...) while((s32[]{:T(128)}, f32[2,153,128]{2,1,0:T(8,128)S(1)}, ...), condition=%wide.region_10.11_spmd.clone, body=%wide.region_7.10_spmd.clone.sunk | while | flops 231664960 | bytes 3280461 | solution.py:150
  192.8 4.8 dynamic_update_slice.74
  206.6 4.8 dynamic_update_slice.74
  220.4 4.8 dynamic_update_slice.74
  234.2 4.8 dynamic_update_slice.74
  248.0 4.8 dynamic_update_slice.74
  261.8 4.8 dynamic_update_slice.74
  275.6 4.8 dynamic_update_slice.74
  289.3 4.8 dynamic_update_slice.74
  299.0 2.4 reshape.237
  301.4 1.9 broadcast_divide_fusion
  306.0 2.8 fusion.81
  310.3 88.0 %all-gather.5.cloned.1.call-done = f32[64,309,128]{2,1,0:T(8,128)} async-done(((f32[1,309,128]{2,1,0:T(8,128)}), f32[64,309,128]{2,1,0:T(8,128)}) %all-gather.5.cloned.1.call-update) | async-done | bytes 10125328 | tf_op jit(solution)/shard_map/all_gather | solution.py:32
  398.3 5.7 copy.304
  408.5 112.2 %while.47 = (s32[]{:T(128)}, f32[2,153,128]{2,1,0:T(8,128)S(1)}, f32[2,153]{1,0:T(2,128)S(1)}, f32[8,2,153,128]{3,2,1,0:T(8,128)}, f32[8,2,153,128]{3,2,1,0:T(8,...) while((s32[]{:T(128)}, f32[2,153,128]{2,1,0:T(8,128)S(1)}, ...), condition=%wide.region_14.15_spmd.clone, body=%wide.region_13.14_spmd.clone.sunk | while | flops 462717824 | bytes 4866477 | solution.py:210
  411.8 2.0 fusion.188
  415.4 2.0 fusion.190
  425.8 2.0 fusion.188
  429.4 2.0 fusion.190
  439.9 2.0 fusion.188
  443.4 2.0 fusion.190
  453.9 1.9 fusion.188
  457.4 2.0 fusion.190
  467.9 2.0 fusion.188
  471.4 2.0 fusion.190
  481.9 2.0 fusion.188
  485.4 2.0 fusion.190
  495.9 1.9 fusion.188
  499.4 2.0 fusion.190
  509.9 1.9 fusion.188
  513.4 2.0 fusion.190
  520.8 2.0 copy.242
  524.5 1.8 copy.243
  526.3 2.0 reshape.243
  529.4 6.0 fusion.85
  535.3 14.0 %scatter_fusion = f32[2,16,1024]{2,0,1:T(2,128)S(1)} fusion(f32[2,16,1024]{2,0,1:T(2,128)S(1)} %split.16, s32[136]{0:T(256)S(1)} %copy-done.16, f32[136,2,1024]{2,1,0:T(2,128)} %get-tuple-element.822), kind=kCustom, calls=%fused_computation.4 | custom fusion | flops 278528 | bytes 3342880 | tf_op jit(solution)/shard_map/transpose(jvp())/scatter-add | solution.py:49
  549.4 7.6 %scatter_fusion.1 = f32[2,16,1024]{2,0,1:T(2,128)S(1)} fusion(f32[2,16,1024]{2,0,1:T(2,128)S(1)} %broadcast.144.clone.1, s32[136]{0:T(256)S(1)} %copy-done.17, f32[136,2,1024]{2,1,0:T(2,128)S(1)} %copy-done.13), kind=kCustom, calls=%fused_computation.5 | custom fusion | flops 278528 | bytes 3342880 | tf_op jit(solution)/shard_map/transpose(jvp())/scatter-add | solution.py:49
  558.4 7.6 %scatter_fusion.3 = f32[2,16,1024]{2,0,1:T(2,128)S(1)} fusion(f32[2,16,1024]{2,0,1:T(2,128)S(1)} %broadcast.144.clone, s32[136]{0:T(256)S(1)} %copy-done.17, f32[136,2,1024]{2,1,0:T(2,128)S(1)} %copy-done.12), kind=kCustom, calls=%fused_computation.7 | custom fusion | flops 278528 | bytes 3342880 | tf_op jit(solution)/shard_map/transpose(jvp())/scatter-add | solution.py:49
  566.0 7.3 scatter_fusion.2
  574.8 3.0 pad_maximum_fusion
  581.3 41.0 %all_to_all.51 = f32[8,128,320]{1,2,0:T(8,128)S(1)} all-to-all(f32[8,128,320]{1,2,0:T(8,128)S(1)} %copy.248), channel_id=1, replica_groups=mesh['seq'=64,'head'=8] {'head'}, dimensions={0} | all-to-all | bytes 2621440 | tf_op jit(solution)/shard_map/all_to_all | solution.py:241
  622.3 2.1 multiply_reduce_fusion.2
  624.9 1.9 collective-permute-start.1
  626.8 95.7 %psum.7 = f32[3,2560]{1,0:T(4,128)} all-reduce(f32[3,2560]{1,0:T(4,128)S(1)} %pad_maximum_fusion.5), channel_id=1, replica_groups=mesh['seq'=64,'head'=8] {'seq','head'}, use_global_device_ids=true, to_apply=%region_22.23 | all-reduce | flops 7680 | bytes 61440 | tf_op jit(solution)/shard_map/psum | solution.py:246
  724.1 4.3 fusion.75
  (397 shorter events, 169.8 us)
Async XLA Ops:
  8.1 8.5 %collective-permute-start = (f32[2,2560]{1,0:T(2,128)S(1)}, f32[2,2560]{1,0:T(2,128)S(1)}, u32[]{:S(2)}, u32[]{:S(2)}) collective-permute-start(f32[2,2560]{1,0:T(2,128)S(1)} %slice.116), channel_id=1, source_target_pairs={{0,1},{1,2},{2,3},{3,4},{4,5},{5,6},{6,7},{7,8},{8,9},{9,10},{10,1... | collective-permute-start | bytes 61448 | tf_op jit(solution)/shard_map/ppermute | solution.py:42
  16.6 3.5 copy-start.3
  17.0 3.1 copy-start.5
  20.1 7.4 %copy-start.17 = (s32[136]{0:T(256)S(1)}, s32[136]{0:T(256)}, u32[]{:S(2)}) copy-start(s32[136]{0:T(256)} %constant.158) | copy-start | bytes 1636
  20.1 7.4 %copy-start.16 = (s32[136]{0:T(256)S(1)}, s32[136]{0:T(256)}, u32[]{:S(2)}) copy-start(s32[136]{0:T(256)} %constant.159) | copy-start | bytes 1636
  20.1 40.9 %all-to-all-start = ((f32[128,8,320]{0,2,1:T(8,128)}), f32[128,8,320]{0,2,1:T(8,128)S(1)}, u32[]{:S(2)}, u32[]{:S(2)}) async-start(f32[128,8,320]{0,2,1:T(8,128)} %bitcast.248), calls=%async_computation | async-start | bytes 2621440 | tf_op jit(solution)/shard_map/all_to_all | solution.py:236
  26.2 153.0 %all-gather.3.cloned.1.call-start = ((), (), s32[]{:S(2)}) async-start(), calls=%async_computation.3 | async-start | bytes 10383360 | tf_op jit(solution)/shard_map/all_gather | solution.py:32
  26.3 66.3 %copy-start.15 = (s32[1026]{0:T(1024)}, s32[1026]{0:T(1024)S(1)}, u32[]{:S(2)}) copy-start(s32[1026]{0:T(1024)S(1)} %select_reduce_fusion) | copy-start | bytes 12316
  74.2 3.0 copy-start.18
  84.9 2.6 copy-start.14
  88.8 32.7 %all-to-all-start.1 = ((f32[128,8,256]{0,2,1:T(8,128)}), f32[128,8,256]{0,2,1:T(8,128)S(1)}, u32[]{:S(2)}, u32[]{:S(2)}) async-start(f32[128,8,256]{0,2,1:T(8,128)} %bitcast.256), calls=%async_computation.1 | async-start | bytes 2097152 | tf_op jit(solution)/shard_map/all_to_all | solution.py:237
  92.4 305.8 %all-gather.5.cloned.1.call-start = ((), (), s32[]{:S(2)}) async-start(), calls=%async_computation.4 | async-start | bytes 10383360 | tf_op jit(solution)/shard_map/all_gather | solution.py:32
  125.5 1.7 copy-start.10
  126.6 1.4 copy-start.9
  187.4 1.3 slice-start.1
  301.4 2.9 copy-start.2
  303.3 1.0 copy-start
  522.8 1.7 copy-start.8
  526.3 3.1 copy-start.7
  528.3 7.1 copy-start.1
  535.3 14.0 %copy-start.13 = (f32[136,2,1024]{2,1,0:T(2,128)S(1)}, f32[136,2,1024]{2,1,0:T(2,128)}, u32[]{:S(2)}) copy-start(f32[136,2,1024]{2,1,0:T(2,128)} %get-tuple-element.821) | copy-start | bytes 3342340
  557.0 1.4 copy-start.12
  558.4 7.6 %slice-start = ((f32[2,153,1024]{2,0,1:T(2,128)}), f32[2,16,1024]{2,0,1:T(2,128)S(1)}, s32[]{:S(2)}) async-start(f32[2,153,1024]{2,0,1:T(2,128)} %copy-done.1), calls=%async_computation.5 | async-start | bytes 262144 | tf_op jit(solution)/shard_map/transpose(jvp())/split | solution.py:51
  558.4 7.6 %copy-start.11 = (f32[136,2,1024]{2,1,0:T(2,128)S(1)}, f32[136,2,1024]{2,1,0:T(2,128)}, u32[]{:S(2)}) copy-start(f32[136,2,1024]{2,1,0:T(2,128)} %get-tuple-element.833) | copy-start | bytes 3342340
  581.3 41.0 %copy-start.4 = (f32[128,2560]{0,1:T(8,128)S(1)}, f32[128,2560]{0,1:T(8,128)}, u32[]{:S(2)}) copy-start(f32[128,2560]{0,1:T(8,128)} %copy-done.3) | copy-start | bytes 3932164
  581.3 41.0 %copy-start.6 = (f32[2,2560]{0,1:T(8,128)S(1)}, f32[2,2560]{0,1:T(8,128)}, u32[]{:S(2)}) copy-start(f32[2,2560]{0,1:T(8,128)} %copy-done.5) | copy-start | bytes 61444
  624.9 97.7 %collective-permute-start.1 = (f32[2,2560]{1,0:T(2,128)S(1)}, f32[2,2560]{1,0:T(2,128)S(1)}, u32[]{:S(2)}, u32[]{:S(2)}) collective-permute-start(f32[2,2560]{1,0:T(2,128)S(1)} %copy.249), channel_id=1, source_target_pairs={{1,0},{2,1},{3,2},{4,3},{5,4},{6,5},{7,6},{8,7},{9,8},{10,9},{11,1... | collective-permute-start | bytes 61448 | tf_op jit(solution)/shard_map/ppermute | solution.py:42
Sparse Core Ops, SparseCore 0:
  87.6 91.5 all-gather.2
  309.7 88.5 all-gather.4
where the time goes:
time: 743 us; the launch traced here: 737 us
  waiting for transfers between devices  198 us (27%)
  local copies, waits for them, and re-layouts  146 us (20%)
  blocking collectives  137 us (18%)
  matrix products  117 us (16%)
  other arithmetic  85.8 us (12%)
  loops' own time  22.4 us (3%)
  starting transfers between devices  15.8 us (2%)
  between operations  15.5 us (2%)
    all_gather x2, waiting for transfers between devices, carried_in(): gathered = lax.all_gather(padded, axis).reshape(lax.axis_size(axis), -1)  136 us
    psum x1, blocking collectives, on_device(): grad_conv = lax.psum(weight_part, ('seq', 'head'))  95.7 us
    dynamic_update_slice x48, local copies, waits for them, and re-layouts, attention_grads(): forward_out = lax.scan(forward_block, (prefix[0], prefix[1]), indices)  55 us
    all_to_all x1, blocking collectives, on_device(): lax.all_to_all(grad_mixed, 'head', split_axis=0, concat_axis=1, tiled=True)  41 us
    all_to_all x1, waiting for transfers between devices, on_device(): lax.all_to_all(outgoing, 'head', split_axis=1, concat_axis=0, tiled=True)  32.9 us
    all_to_all x1, waiting for transfers between devices, on_device(): lax.all_to_all(out_grads, 'head', split_axis=1, concat_axis=0, tiled=True)  28.9 us
    unnamed x48, local copies, waits for them, and re-layouts  23.9 us
    scatter-add x2, other arithmetic, feature_map(): columns[:, upper_j, :]  21.3 us
  transfers between devices with their start and end apart: 6, of which 4 were waited for; matrix products, arithmetic and copies ran while one was open for 2% of the time, Pallas kernels for 0%

commit v1 on v0

--- a/solution.py
+++ b/solution.py
@@ -243,7 +243,8 @@
     grad_projected, weight_part = conv_backward(
         returned, trailing, projected, leading, conv_weight, token_offsets
     )
-    grad_conv = lax.psum(weight_part, ("seq", "head"))
+    inner = lax.psum(weight_part, "seq")
+    grad_conv = lax.psum(inner, "head")
     return (grad_projected, grad_conv)
 
 

time: 743 us -> 921 us (1.24)
  blocking collectives: 137 us -> 305 us
    psum x1 -> x2, blocking collectives: 95.7 us -> 264 us  [the longest x1 243 us: on_device(): inner = lax.psum(weight_part, 'seq')]
where the time goes in v1:
time: 921 us; the launch traced here: 907 us
  blocking collectives  305 us (33%)
  waiting for transfers between devices  198 us (21%)
  local copies, waits for them, and re-layouts  146 us (16%)
  matrix products  117 us (13%)
  other arithmetic  85.8 us (9%)
  loops' own time  22.4 us (2%)
  starting transfers between devices  17.9 us (2%)
  between operations  15.5 us (2%)
    psum x1, blocking collectives, on_device(): inner = lax.psum(weight_part, 'seq')  243 us
    all_gather x2, waiting for transfers between devices, carried_in(): gathered = lax.all_gather(padded, axis).reshape(lax.axis_size(axis), -1)  136 us
    dynamic_update_slice x48, local copies, waits for them, and re-layouts, attention_grads(): forward_out = lax.scan(forward_block, (prefix[0], prefix[1]), indices)  55 us
    all_to_all x1, blocking collectives, on_device(): lax.all_to_all(grad_mixed, 'head', split_axis=0, concat_axis=1, tiled=True)  41 us
    all_to_all x1, waiting for transfers between devices, on_device(): lax.all_to_all(outgoing, 'head', split_axis=1, concat_axis=0, tiled=True)  32.9 us
    all_to_all x1, waiting for transfers between devices, on_device(): lax.all_to_all(out_grads, 'head', split_axis=1, concat_axis=0, tiled=True)  28.9 us
    unnamed x48, local copies, waits for them, and re-layouts  23.9 us
    scatter-add x2, other arithmetic, feature_map(): columns[:, upper_j, :]  21.3 us
  transfers between devices with their start and end apart: 6, of which 4 were waited for; matrix products, arithmetic and copies ran while one was open for 2% of the time, Pallas kernels for 0%

profile of v1, /device:TPU:1, one launch (start us, length us, event | category | flops | bytes accessed | tf_op | source)
XLA Modules:
  0.0 907.4 jit_solution(11089164403028575608)
XLA Ops:
  8.1 4.0 collective-permute-start
  17.0 3.1 multiply_add_fusion.1
  20.1 6.1 all-to-all-start
  28.1 32.9 %all-to-all-done = f32[128,8,320]{0,2,1:T(8,128)S(1)} async-done(((f32[128,8,320]{0,2,1:T(8,128)}), f32[128,8,320]{0,2,1:T(8,128)S(1)}, u32[]{:S(2)}, u32[]{:S(2)}) %all-to-all-start) | async-done | bytes 1310752 | tf_op jit(solution)/shard_map/all_to_all | solution.py:236
  61.0 1.8 copy.225
  62.8 2.0 reshape.227
  65.0 3.0 gather_fusion
  68.1 3.1 gather_fusion.1
  71.1 3.0 gather_fusion.2
  74.2 3.0 gather_fusion.3
  77.2 3.4 fusion.89
  80.6 4.3 fusion.98
  88.8 3.6 all-to-all-start.1
  92.7 28.9 %all-to-all-done.1 = f32[128,8,256]{0,2,1:T(8,128)S(1)} async-done(((f32[128,8,256]{0,2,1:T(8,128)}), f32[128,8,256]{0,2,1:T(8,128)S(1)}, u32[]{:S(2)}, u32[]{:S(2)}) %all-to-all-start.1) | async-done | bytes 1048608 | tf_op jit(solution)/shard_map/all_to_all | solution.py:237
  123.2 2.4 reshape.233
  128.4 2.5 copy.272
  131.0 48.2 %all-gather.3.cloned.1.call-done = f32[64,309,128]{2,1,0:T(8,128)} async-done(((f32[1,309,128]{2,1,0:T(8,128)}), f32[64,309,128]{2,1,0:T(8,128)}) %all-gather.3.cloned.1.call-update) | async-done | bytes 10125328 | tf_op jit(solution)/shard_map/all_gather | solution.py:32
  179.2 5.7 copy.305
  188.8 110.3 %while.46 = (s32[]{:T(128)}, f32[2,153,128]{2,1,0:T(8,128)S(1)}, f32[2,153]{1,0:T(2,128)S(1)}, f32[8,128,2,128]{1,0,3,2:T(8,128)}, f32[8,2,128]{2,1,0:T(2,128)S(...) while((s32[]{:T(128)}, f32[2,153,128]{2,1,0:T(8,128)S(1)}, ...), condition=%wide.region_10.11_spmd.clone, body=%wide.region_7.10_spmd.clone.sunk | while | flops 231664960 | bytes 3280461 | solution.py:150
  192.8 4.8 dynamic_update_slice.74
  206.6 4.8 dynamic_update_slice.74
  220.4 4.8 dynamic_update_slice.74
  234.2 4.8 dynamic_update_slice.74
  248.0 4.8 dynamic_update_slice.74
  261.8 4.8 dynamic_update_slice.74
  275.6 4.8 dynamic_update_slice.74
  289.3 4.8 dynamic_update_slice.74
  299.0 2.4 reshape.237
  301.4 1.9 broadcast_divide_fusion
  306.0 2.8 fusion.81
  310.3 88.0 %all-gather.5.cloned.1.call-done = f32[64,309,128]{2,1,0:T(8,128)} async-done(((f32[1,309,128]{2,1,0:T(8,128)}), f32[64,309,128]{2,1,0:T(8,128)}) %all-gather.5.cloned.1.call-update) | async-done | bytes 10125328 | tf_op jit(solution)/shard_map/all_gather | solution.py:32
  398.3 5.7 copy.304
  408.5 112.2 %while.47 = (s32[]{:T(128)}, f32[2,153,128]{2,1,0:T(8,128)S(1)}, f32[2,153]{1,0:T(2,128)S(1)}, f32[8,2,153,128]{3,2,1,0:T(8,128)}, f32[8,2,153,128]{3,2,1,0:T(8,...) while((s32[]{:T(128)}, f32[2,153,128]{2,1,0:T(8,128)S(1)}, ...), condition=%wide.region_14.15_spmd.clone, body=%wide.region_13.14_spmd.clone.sunk | while | flops 462717824 | bytes 4866477 | solution.py:210
  411.8 2.0 fusion.188
  415.4 2.0 fusion.190
  425.8 2.0 fusion.188
  429.4 2.0 fusion.190
  439.9 2.0 fusion.188
  443.4 2.0 fusion.190
  453.9 1.9 fusion.188
  457.4 2.0 fusion.190
  467.9 2.0 fusion.188
  471.4 2.0 fusion.190
  481.9 2.0 fusion.188
  485.4 2.0 fusion.190
  495.9 1.9 fusion.188
  499.4 2.0 fusion.190
  509.9 1.9 fusion.188
  513.4 2.0 fusion.190
  520.8 2.0 copy.242
  524.5 1.8 copy.243
  526.3 2.0 reshape.243
  529.4 6.0 fusion.85
  535.3 14.0 %scatter_fusion = f32[2,16,1024]{2,0,1:T(2,128)S(1)} fusion(f32[2,16,1024]{2,0,1:T(2,128)S(1)} %split.16, s32[136]{0:T(256)S(1)} %copy-done.16, f32[136,2,1024]{2,1,0:T(2,128)} %get-tuple-element.822), kind=kCustom, calls=%fused_computation.4 | custom fusion | flops 278528 | bytes 3342880 | tf_op jit(solution)/shard_map/transpose(jvp())/scatter-add | solution.py:49
  549.4 7.6 scatter_fusion.1
  558.4 7.6 scatter_fusion.3
  566.0 7.3 scatter_fusion.2
  574.8 3.0 pad_maximum_fusion
  581.3 41.0 %all_to_all.51 = f32[8,128,320]{1,2,0:T(8,128)S(1)} all-to-all(f32[8,128,320]{1,2,0:T(8,128)S(1)} %copy.248), channel_id=1, replica_groups=mesh['seq'=64,'head'=8] {'head'}, dimensions={0} | all-to-all | bytes 2621440 | tf_op jit(solution)/shard_map/all_to_all | solution.py:241
  622.3 2.1 multiply_reduce_fusion.2
  624.5 243.1 %psum.14 = f32[3,2560]{1,0:T(4,128)S(1)} all-reduce(f32[3,2560]{1,0:T(4,128)S(1)} %pad_maximum_fusion.5), channel_id=1, replica_groups=mesh['seq'=64,'head'=8] {'seq'}, use_global_device_ids=true, to_apply=%region_22.23 | all-reduce | flops 7680 | bytes 61440 | tf_op jit(solution)/shard_map/psum | solution.py:246
  868.0 4.0 collective-permute-start.1
  871.9 21.0 %psum.15 = f32[3,2560]{1,0:T(4,128)} all-reduce(f32[3,2560]{1,0:T(4,128)S(1)} %psum.14), channel_id=1, replica_groups=mesh['seq'=64,'head'=8] {'head'}, use_global_device_ids=true, to_apply=%region_23.24 | all-reduce | flops 7680 | bytes 61440 | tf_op jit(solution)/shard_map/psum | solution.py:247
  894.5 4.3 fusion.75
  (398 shorter events, 171.5 us)
Async XLA Ops:
  8.1 8.5 collective-permute-start
  16.6 3.5 copy-start.3
  17.0 3.1 copy-start.5
  20.1 7.4 copy-start.17
  20.1 7.4 copy-start.16
  20.1 40.9 %all-to-all-start = ((f32[128,8,320]{0,2,1:T(8,128)}), f32[128,8,320]{0,2,1:T(8,128)S(1)}, u32[]{:S(2)}, u32[]{:S(2)}) async-start(f32[128,8,320]{0,2,1:T(8,128)} %bitcast.248), calls=%async_computation | async-start | bytes 2621440 | tf_op jit(solution)/shard_map/all_to_all | solution.py:236
  26.2 153.0 %all-gather.3.cloned.1.call-start = ((), (), s32[]{:S(2)}) async-start(), calls=%async_computation.3 | async-start | bytes 10383360 | tf_op jit(solution)/shard_map/all_gather | solution.py:32
  26.3 66.3 %copy-start.15 = (s32[1026]{0:T(1024)}, s32[1026]{0:T(1024)S(1)}, u32[]{:S(2)}) copy-start(s32[1026]{0:T(1024)S(1)} %select_reduce_fusion) | copy-start | bytes 12316
  74.2 3.0 copy-start.18
  84.9 2.6 copy-start.14
  88.8 32.7 %all-to-all-start.1 = ((f32[128,8,256]{0,2,1:T(8,128)}), f32[128,8,256]{0,2,1:T(8,128)S(1)}, u32[]{:S(2)}, u32[]{:S(2)}) async-start(f32[128,8,256]{0,2,1:T(8,128)} %bitcast.256), calls=%async_computation.1 | async-start | bytes 2097152 | tf_op jit(solution)/shard_map/all_to_all | solution.py:237
  92.4 305.8 %all-gather.5.cloned.1.call-start = ((), (), s32[]{:S(2)}) async-start(), calls=%async_computation.4 | async-start | bytes 10383360 | tf_op jit(solution)/shard_map/all_gather | solution.py:32
  125.5 1.7 copy-start.10
  126.6 1.4 copy-start.9
  187.4 1.3 slice-start.1
  301.4 2.9 copy-start.2
  303.3 1.0 copy-start
  522.8 1.7 copy-start.8
  526.3 3.1 copy-start.7
  528.3 7.1 copy-start.1
  535.3 14.0 %copy-start.13 = (f32[136,2,1024]{2,1,0:T(2,128)S(1)}, f32[136,2,1024]{2,1,0:T(2,128)}, u32[]{:S(2)}) copy-start(f32[136,2,1024]{2,1,0:T(2,128)} %get-tuple-element.821) | copy-start | bytes 3342340
  557.0 1.4 copy-start.12
  558.4 7.6 slice-start
  558.4 7.6 copy-start.11
  581.3 41.0 %copy-start.4 = (f32[128,2560]{0,1:T(8,128)S(1)}, f32[128,2560]{0,1:T(8,128)}, u32[]{:S(2)}) copy-start(f32[128,2560]{0,1:T(8,128)} %copy-done.3) | copy-start | bytes 3932164
  581.3 41.0 %copy-start.6 = (f32[2,2560]{0,1:T(8,128)S(1)}, f32[2,2560]{0,1:T(8,128)}, u32[]{:S(2)}) copy-start(f32[2,2560]{0,1:T(8,128)} %copy-done.5) | copy-start | bytes 61444
  868.0 25.0 %collective-permute-start.1 = (f32[2,2560]{1,0:T(2,128)S(1)}, f32[2,2560]{1,0:T(2,128)S(1)}, u32[]{:S(2)}, u32[]{:S(2)}) collective-permute-start(f32[2,2560]{1,0:T(2,128)S(1)} %copy.249), channel_id=1, source_target_pairs={{1,0},{2,1},{3,2},{4,3},{5,4},{6,5},{7,6},{8,7},{9,8},{10,9},{11,1... | collective-permute-start | bytes 61448 | tf_op jit(solution)/shard_map/ppermute | solution.py:42
Sparse Core Ops, SparseCore 0:
  87.6 91.5 all-gather.2
  309.7 88.5 all-gather.4
